TPU v7x, 32 devices: a whole 2x2x4 slice. The times are simulated.
32 devices in a mesh: blk: 8 (over z, x), cent: 4 (over y, core).
Axes of the slice: x: 2, y: 2, z: 4, core: 2. Of those that a mesh axis runs over, the one named last changes fastest.
Arguments:
- descriptors: bfloat16 [6144, 1024], P('blk'), may hold values from -6 to 6
- landmarks: bfloat16 [4096, 1024], P('blk'), may hold values from -6 to 6
- whitening: bfloat16 [4096, 4096], P('blk', 'cent'), may hold values from -0.09375 to 0.09375
- centroids: bfloat16 [4096, 4096], P('cent'), may hold values from -8 to 8, as said below
Outputs:
- assign: bfloat16 [6144, 4096], P('blk', 'cent')
- new_centroids: float32 [4096, 4096], P('blk', 'cent')
Inputs may be any that keep to these rules, and one draw needn't show every extreme that they name: `centroids`: centroid coordinates.
All inputs are finite; a program needn't handle non-finite values.
Results may differ from a plain program's by a relative error of at most 0.03.
Values may be sent and summed in bfloat16 or wider, within the bound.
No kernel may reach another device: no remote copies, remote signals or barrier semaphores. Data moves between devices by JAX's collectives and lax.ppermute only.
A program may use at most 128 MiB of HBM per device.

v0:
```python
import math
import jax
import jax.numpy as jnp
from jax import lax
from jax.sharding import PartitionSpec as P


def unit_rows(values):
    wide = values.astype(jnp.float32)
    sum_sq = jnp.sum(wide * wide, axis=1, keepdims=True)
    scale = lax.rsqrt(sum_sq + 1e-06)
    return (wide * scale).astype(jnp.bfloat16)


def per_device(descriptors, landmarks, whitening, centroids):
    unit_desc = unit_rows(descriptors)
    unit_land = unit_rows(landmarks)
    sharpness = math.sqrt(descriptors.shape[1])
    cosine = lax.dot_general(
        unit_desc,
        lax.all_gather(unit_land, "blk", axis=0, tiled=True),
        (((1,), (1,)), ((), ())),
        preferred_element_type=jnp.float32,
    )
    kernel = jnp.exp(sharpness * cosine).astype(jnp.bfloat16)
    feature_cols = jnp.dot(
        kernel,
        lax.all_gather(whitening, "blk", axis=0, tiled=True),
        preferred_element_type=jnp.float32,
    )
    features = lax.all_gather(feature_cols.astype(jnp.bfloat16), "cent", axis=1, tiled=True)
    logits = lax.dot_general(
        features, centroids, (((1,), (1,)), ((), ())), preferred_element_type=jnp.float32
    )
    local_top = jnp.max(logits, axis=1)
    row_top = lax.pmax(local_top, "cent")
    weights = jnp.exp(logits - row_top[:, None])
    row_total = lax.psum(jnp.sum(weights, axis=1), "cent")
    assign = (weights / row_total[:, None]).astype(jnp.bfloat16)
    counts = lax.psum(jnp.sum(assign.astype(jnp.float32), axis=0), "blk")
    sums = lax.psum_scatter(
        lax.dot_general(
            features, assign, (((0,), (0,)), ((), ())), preferred_element_type=jnp.float32
        ).astype(jnp.bfloat16),
        "blk",
        scatter_dimension=0,
        tiled=True,
    ).astype(jnp.float32)
    return (assign, sums / jnp.maximum(counts, 1.0)[None, :])


def solution(mesh):
    in_specs = (P("blk", None), P("blk", None), P("blk", "cent"), P("cent", None))
    out_specs = (P("blk", "cent"), P("blk", "cent"))
    return jax.shard_map(
        per_device, mesh=mesh, in_specs=in_specs, out_specs=out_specs, check_vma=False
    )
```

profile of v0, /device:TPU:0, one launch (start us, length us, event | category | flops | bytes accessed | tf_op | source)
XLA Modules:
  0.0 523.7 jit_solution(12697928453037709906)
XLA Ops:
  7.2 0.0 copy-start
  7.2 0.0 all-gather.6.cloned.1.call-start
  7.2 0.7 all-gather.6.cloned.1.call-update
  7.9 0.0 all-gather.4.cloned.1.call-start
  8.0 1.5 fusion.3
  9.5 2.4 fusion.4
  11.9 0.0 all-gather.4.cloned.1.call-update
  11.9 0.0 all-gather.8.cloned.1.call-start
  12.0 0.0 copy-done
  12.0 0.4 fusion
  12.4 125.0 %all-gather.6.cloned.1.call-done = bf16[4096,1024]{1,0:T(8,128)(2,1)} async-done(((bf16[512,1024]{1,0:T(8,128)(2,1)}), bf16[4096,1024]{1,0:T(8,128)(2,1)}) %all-gather.6.cloned.1.call-update) | async-done | bytes 8388624 | tf_op jit(solution)/shard_map/all_gather | solution.py:28
  137.3 125.4 %all-gather.4.cloned.1.call-done = bf16[4096,1024]{1,0:T(8,128)(2,1)} async-done(((bf16[512,1024]{1,0:T(8,128)(2,1)}), bf16[4096,1024]{1,0:T(8,128)(2,1)}) %all-gather.4.cloned.1.call-update) | async-done | bytes 8388624 | tf_op jit(solution)/shard_map/all_gather | solution.py:21
  262.7 20.2 %convolution_convert_fusion.1 = bf16[768,1024]{1,0:T(8,128)(2,1)} fusion(bf16[4096,1024]{1,0:T(8,128)(2,1)} %all-gather.6.cloned.1.call-done, bf16[4096,1024]{1,0:T(8,128)(2,1)} %all-gather.4.cloned.1.call-done, bf16[768,1024]{1,0:T(8,128)(2,1)S(1)} %copy-done, f32[768]{0:T(1024)S(1)} %add_rsqrt_fusion), kind=kOutput, calls=%fused_computation.15 | convolution fusion | flops 12894339072 | bytes 19926016 | tf_op jit(solution)/shard_map/dot_general | solution.py:26
  282.9 0.0 all-gather.8.cloned.1.call-update
  282.9 0.2 reduce-scatter.2.cloned.1.call-start
  283.1 44.5 %all-gather.8.cloned.1.call-done = bf16[768,4096]{1,0:T(8,128)(2,1)} async-done(((bf16[768,1024]{1,0:T(8,128)(2,1)}), bf16[768,4096]{1,0:T(8,128)(2,1)}) %all-gather.8.cloned.1.call-update) | async-done | bytes 6291472 | tf_op jit(solution)/shard_map/all_gather | solution.py:31
  327.6 11.1 %fusion.11 = (f32[768]{0:T(1024)S(1)}, f32[768,1024]{1,0:T(8,128)S(1)}) fusion(bf16[768,4096]{1,0:T(8,128)(2,1)} %all-gather.8.cloned.1.call-done, bf16[1024,4096]{1,0:T(8,128)(2,1)} %param.7), kind=kOutput, calls=%fused_computation.21 | convolution fusion | flops 6443236352 | bytes 17828864 | tf_op jit(solution)/shard_map/dot_general | solution.py:32
  338.7 5.9 %pmax.7 = f32[768]{0:T(1024)S(1)} all-reduce(f32[768]{0:T(1024)S(1)} %get-tuple-element.4), channel_id=1, replica_groups=mesh['blk'=8,'cent'=4] {'cent'}, use_global_device_ids=true, to_apply=%region_3.0 | all-reduce | flops 768 | bytes 6144 | tf_op jit(solution)/shard_map/pmax | solution.py:36
  344.6 0.9 fusion.2
  345.6 5.7 %psum.14 = f32[768]{0:T(1024)S(1)} all-reduce(f32[768]{0:T(1024)S(1)} %fusion.2), channel_id=1, replica_groups=mesh['blk'=8,'cent'=4] {'cent'}, use_global_device_ids=true, to_apply=%region_5.0 | all-reduce | flops 768 | bytes 6144 | tf_op jit(solution)/shard_map/psum | solution.py:38
  351.2 1.0 convert_reduce_fusion
  352.2 0.0 copy-start.1
  352.2 1.1 copy-done.1
  353.4 11.9 %convolution_convert_fusion = bf16[4096,1024]{1,0:T(8,128)(2,1)} fusion(bf16[768,4096]{1,0:T(8,128)(2,1)} %all-gather.8.cloned.1.call-done, bf16[768,1024]{1,0:T(8,128)(2,1)S(1)} %get-tuple-element.3), kind=kOutput, calls=%fused_computation.1 | convolution fusion | flops 6446645248 | bytes 16252928 | tf_op jit(solution)/shard_map/dot_general | solution.py:42
  365.2 0.0 reduce-scatter.2.cloned.1.call-update
  365.3 22.1 %psum.15 = f32[1024]{0:T(1024)S(1)} all-reduce(f32[1024]{0:T(1024)S(1)} %get-tuple-element.2), channel_id=1, replica_groups=mesh['blk'=8,'cent'=4] {'blk'}, use_global_device_ids=true, to_apply=%region_8.0 | all-reduce | flops 1024 | bytes 8192 | tf_op jit(solution)/shard_map/psum | solution.py:40
  387.4 127.0 %reduce-scatter.2.cloned.1.call-done = bf16[512,1024]{1,0:T(8,128)(2,1)} async-done(((bf16[4096,1024]{1,0:T(8,128)(2,1)}), bf16[512,1024]{1,0:T(8,128)(2,1)}) %reduce-scatter.2.cloned.1.call-update) | async-done | bytes 1048592 | tf_op jit(solution)/shard_map/reduce_scatter | solution.py:41
  514.3 2.9 convert_divide_fusion
  (3 shorter events, 0.0 us)
Async XLA Ops:
  7.2 4.8 copy-start
  7.2 130.2 %all-gather.6.cloned.1.call-start = ((), (), s32[]{:S(2)}) async-start(), calls=%async_computation.2 | async-start | bytes 9437184 | tf_op jit(solution)/shard_map/all_gather | solution.py:28
  7.9 254.8 %all-gather.4.cloned.1.call-start = ((), (), s32[]{:S(2)}) async-start(), calls=%async_computation.1 | async-start | bytes 9437184 | tf_op jit(solution)/shard_map/all_gather | solution.py:21
  11.9 315.7 %all-gather.8.cloned.1.call-start = ((), (), s32[]{:S(2)}) async-start(), calls=%async_computation.3 | async-start | bytes 7864320 | tf_op jit(solution)/shard_map/all_gather | solution.py:31
  282.9 231.4 %reduce-scatter.2.cloned.1.call-start = ((), (), s32[]{:S(2)}) async-start(), calls=%async_computation.4 | async-start | bytes 9437184 | tf_op jit(solution)/shard_map/reduce_scatter | solution.py:41
  352.2 1.1 copy-start.1
Sparse Core Ops, SparseCore 0:
  10.1 127.1 all-gather.5
  140.0 122.6 all-gather.3
  283.0 44.5 all-gather.7
  365.4 148.9 reduce-scatter.1
where the time goes:
time: 524 us
  waiting for transfers between devices  423 us (81%)
  matrix products  43.2 us (8%)
  blocking collectives  33.7 us (6%)
  between operations  13.8 us (3%)
  other arithmetic  9.08 us (2%)
    reduce_scatter x1, waiting for transfers between devices, per_device(): lax.psum_scatter(lax.dot_general(features, assign, (((0,), (0,)), ((), ()...  127 us
    all_gather x1, waiting for transfers between devices, per_device(): lax.all_gather(unit_land, 'blk', axis=0, tiled=True)  125 us
    all_gather x1, waiting for transfers between devices, per_device(): lax.all_gather(whitening, 'blk', axis=0, tiled=True)  125 us
    all_gather x1, waiting for transfers between devices, per_device(): lax.all_gather(feature_cols.astype(jnp.bfloat16), 'cent', axis=1, tiled=T...  44.5 us
    psum x1, blocking collectives, per_device(): counts = lax.psum(jnp.sum(assign.astype(jnp.float32), axis=0), 'blk')  22.1 us
    dot_general x1, matrix products, per_device(): jnp.dot(kernel, lax.all_gather(whitening, 'blk', axis=0, tiled=True), pre...  20.2 us
    dot_general x1, matrix products, per_device(): lax.dot_general(features, assign, (((0,), (0,)), ((), ())), preferred_ele...  11.9 us
    dot_general x1, matrix products, per_device(): lax.dot_general(features, centroids, (((1,), (1,)), ((), ())), preferred_...  11.1 us
  transfers between devices with their start and end apart: 4, of which 4 were waited for; matrix products, arithmetic and copies ran while one was open for 1% of the time, Pallas kernels for 0%

commit v1 on v0

--- a/solution.py
+++ b/solution.py
@@ -37,7 +37,7 @@
     weights = jnp.exp(logits - row_top[:, None])
     row_total = lax.psum(jnp.sum(weights, axis=1), "cent")
     assign = (weights / row_total[:, None]).astype(jnp.bfloat16)
-    counts = lax.psum(jnp.sum(assign.astype(jnp.float32), axis=0), "blk")
+    counts = jnp.sum(lax.all_gather(jnp.sum(assign.astype(jnp.float32), axis=0), "blk"), axis=0)
     sums = lax.psum_scatter(
         lax.dot_general(
             features, assign, (((0,), (0,)), ((), ())), preferred_element_type=jnp.float32

time: 524 us -> 524 us (level)
  waiting for transfers between devices: 423 us -> 413 us
  blocking collectives: 33.7 us -> 43.4 us
    all_gather x0 -> x1, blocking collectives: none -> 31.8 us  [per_device(): lax.all_gather(jnp.sum(assign.astype(jnp.float32), axis=0), 'blk')]
    psum x1 -> x0, blocking collectives: 22.1 us -> none  [per_device(): counts = lax.psum(jnp.sum(assign.astype(jnp.float32), axis=0), 'blk')]
    reduce_scatter x1, waiting for transfers between devices: 127 us -> 117 us  [per_device(): lax.psum_scatter(lax.dot_general(features, assign, (((0,), (0,)), ((), ()...]
where the time goes in v1:
time: 524 us
  waiting for transfers between devices  413 us (79%)
  blocking collectives  43.4 us (8%)
  matrix products  43.2 us (8%)
  between operations  13.8 us (3%)
  other arithmetic  9.1 us (2%)
    all_gather x1, waiting for transfers between devices, per_device(): lax.all_gather(unit_land, 'blk', axis=0, tiled=True)  125 us
    all_gather x1, waiting for transfers between devices, per_device(): lax.all_gather(whitening, 'blk', axis=0, tiled=True)  125 us
    reduce_scatter x1, waiting for transfers between devices, per_device(): lax.psum_scatter(lax.dot_general(features, assign, (((0,), (0,)), ((), ()...  117 us
    all_gather x1, waiting for transfers between devices, per_device(): lax.all_gather(feature_cols.astype(jnp.bfloat16), 'cent', axis=1, tiled=T...  44.5 us
    all_gather x1, blocking collectives, per_device(): lax.all_gather(jnp.sum(assign.astype(jnp.float32), axis=0), 'blk')  31.8 us
    dot_general x1, matrix products, per_device(): jnp.dot(kernel, lax.all_gather(whitening, 'blk', axis=0, tiled=True), pre...  20.2 us
    dot_general x1, matrix products, per_device(): lax.dot_general(features, assign, (((0,), (0,)), ((), ())), preferred_ele...  11.9 us
    dot_general x1, matrix products, per_device(): lax.dot_general(features, centroids, (((1,), (1,)), ((), ())), preferred_...  11.1 us
  transfers between devices with their start and end apart: 4, of which 4 were waited for; matrix products, arithmetic and copies ran while one was open for 1% of the time, Pallas kernels for 0%

profile of v1, /device:TPU:0, one launch (start us, length us, event | category | flops | bytes accessed | tf_op | source)
XLA Modules:
  0.0 523.8 jit_solution(13222251277046482189)
XLA Ops:
  7.2 0.0 copy-start
  7.2 0.0 all-gather.7.cloned.1.call-start
  7.2 0.7 all-gather.7.cloned.1.call-update
  7.9 0.0 all-gather.5.cloned.1.call-start
  8.0 1.5 fusion.3
  9.5 2.4 fusion.4
  11.9 0.0 all-gather.5.cloned.1.call-update
  11.9 0.0 all-gather.9.cloned.1.call-start
  12.0 0.0 copy-done
  12.0 0.4 fusion
  12.4 125.0 %all-gather.7.cloned.1.call-done = bf16[4096,1024]{1,0:T(8,128)(2,1)} async-done(((bf16[512,1024]{1,0:T(8,128)(2,1)}), bf16[4096,1024]{1,0:T(8,128)(2,1)}) %all-gather.7.cloned.1.call-update) | async-done | bytes 8388624 | tf_op jit(solution)/shard_map/all_gather | solution.py:28
  137.3 125.4 %all-gather.5.cloned.1.call-done = bf16[4096,1024]{1,0:T(8,128)(2,1)} async-done(((bf16[512,1024]{1,0:T(8,128)(2,1)}), bf16[4096,1024]{1,0:T(8,128)(2,1)}) %all-gather.5.cloned.1.call-update) | async-done | bytes 8388624 | tf_op jit(solution)/shard_map/all_gather | solution.py:21
  262.7 20.2 %convolution_convert_fusion.1 = bf16[768,1024]{1,0:T(8,128)(2,1)} fusion(bf16[4096,1024]{1,0:T(8,128)(2,1)} %all-gather.7.cloned.1.call-done, bf16[4096,1024]{1,0:T(8,128)(2,1)} %all-gather.5.cloned.1.call-done, bf16[768,1024]{1,0:T(8,128)(2,1)S(1)} %copy-done, f32[768]{0:T(1024)S(1)} %add_rsqrt_fusion), kind=kOutput, calls=%fused_computation.15 | convolution fusion | flops 12894339072 | bytes 19926016 | tf_op jit(solution)/shard_map/dot_general | solution.py:26
  282.9 0.0 all-gather.9.cloned.1.call-update
  282.9 0.2 reduce-scatter.2.cloned.1.call-start
  283.1 44.5 %all-gather.9.cloned.1.call-done = bf16[768,4096]{1,0:T(8,128)(2,1)} async-done(((bf16[768,1024]{1,0:T(8,128)(2,1)}), bf16[768,4096]{1,0:T(8,128)(2,1)}) %all-gather.9.cloned.1.call-update) | async-done | bytes 6291472 | tf_op jit(solution)/shard_map/all_gather | solution.py:31
  327.6 11.1 %fusion.11 = (f32[768]{0:T(1024)S(1)}, f32[768,1024]{1,0:T(8,128)S(1)}) fusion(bf16[768,4096]{1,0:T(8,128)(2,1)} %all-gather.9.cloned.1.call-done, bf16[1024,4096]{1,0:T(8,128)(2,1)} %param.7), kind=kOutput, calls=%fused_computation.21 | convolution fusion | flops 6443236352 | bytes 17828864 | tf_op jit(solution)/shard_map/dot_general | solution.py:32
  338.7 5.9 %pmax.7 = f32[768]{0:T(1024)S(1)} all-reduce(f32[768]{0:T(1024)S(1)} %get-tuple-element.4), channel_id=1, replica_groups=mesh['blk'=8,'cent'=4] {'cent'}, use_global_device_ids=true, to_apply=%region_3.0 | all-reduce | flops 768 | bytes 6144 | tf_op jit(solution)/shard_map/pmax | solution.py:36
  344.6 0.9 fusion.2
  345.6 5.7 %psum.7 = f32[768]{0:T(1024)S(1)} all-reduce(f32[768]{0:T(1024)S(1)} %fusion.2), channel_id=1, replica_groups=mesh['blk'=8,'cent'=4] {'cent'}, use_global_device_ids=true, to_apply=%region_5.0 | all-reduce | flops 768 | bytes 6144 | tf_op jit(solution)/shard_map/psum | solution.py:38
  351.2 1.0 convert_reduce_fusion
  352.2 0.0 copy-start.1
  352.2 1.1 copy-done.1
  353.4 11.9 %convolution_convert_fusion = bf16[4096,1024]{1,0:T(8,128)(2,1)} fusion(bf16[768,4096]{1,0:T(8,128)(2,1)} %all-gather.9.cloned.1.call-done, bf16[768,1024]{1,0:T(8,128)(2,1)S(1)} %get-tuple-element.3), kind=kOutput, calls=%fused_computation.1 | convolution fusion | flops 6446645248 | bytes 16252928 | tf_op jit(solution)/shard_map/dot_general | solution.py:42
  365.2 0.0 reduce-scatter.2.cloned.1.call-update
  365.3 31.8 %all-gather = f32[8192]{0:T(1024)S(1)} all-gather(f32[1024]{0:T(1024)S(1)} %get-tuple-element.2), channel_id=2, replica_groups=mesh['blk'=8,'cent'=4] {'blk'}, dimensions={0}, use_global_device_ids=true | all-gather | bytes 36864 | tf_op jit(solution)/shard_map/all_gather | solution.py:40
  397.1 117.3 %reduce-scatter.2.cloned.1.call-done = bf16[512,1024]{1,0:T(8,128)(2,1)} async-done(((bf16[4096,1024]{1,0:T(8,128)(2,1)}), bf16[512,1024]{1,0:T(8,128)(2,1)}) %reduce-scatter.2.cloned.1.call-update) | async-done | bytes 1048592 | tf_op jit(solution)/shard_map/reduce_scatter | solution.py:41
  514.4 2.9 convert_divide_fusion
  (5 shorter events, 0.0 us)
Async XLA Ops:
  7.2 4.8 copy-start
  7.2 130.2 %all-gather.7.cloned.1.call-start = ((), (), s32[]{:S(2)}) async-start(), calls=%async_computation.2 | async-start | bytes 9437184 | tf_op jit(solution)/shard_map/all_gather | solution.py:28
  7.9 254.8 %all-gather.5.cloned.1.call-start = ((), (), s32[]{:S(2)}) async-start(), calls=%async_computation.1 | async-start | bytes 9437184 | tf_op jit(solution)/shard_map/all_gather | solution.py:21
  11.9 315.7 %all-gather.9.cloned.1.call-start = ((), (), s32[]{:S(2)}) async-start(), calls=%async_computation.3 | async-start | bytes 7864320 | tf_op jit(solution)/shard_map/all_gather | solution.py:31
  282.9 231.5 %reduce-scatter.2.cloned.1.call-start = ((), (), s32[]{:S(2)}) async-start(), calls=%async_computation.4 | async-start | bytes 9437184 | tf_op jit(solution)/shard_map/reduce_scatter | solution.py:41
  352.2 1.1 copy-start.1
Sparse Core Ops, SparseCore 0:
  10.1 127.1 all-gather.6
  140.0 122.6 all-gather.4
  283.0 44.5 all-gather.8
  365.4 148.9 reduce-scatter.1
